TPU v7x, 128 devices: a whole 4x4x4 slice. The times are simulated.
128 devices in a mesh: req: 16 (over y, x), head: 8 (over z, core).
Axes of the slice: x: 4, y: 4, z: 4, core: 2. Of those that a mesh axis runs over, the one named last changes fastest.
Arguments:
- hidden_in: bfloat16 [4864, 3072], P('req', 'head'), may hold values from -6 to 6
- dec_query: bfloat16 [768, 3072], P('req', 'head'), may hold values from -5.5 to 5.5
- dec_key: bfloat16 [768, 3072], P('req', 'head'), may hold values from -6 to 6
- dec_value: bfloat16 [768, 3072], P('req', 'head'), may hold values from -6 to 6
- pre_query: bfloat16 [4096, 3072], P('req', 'head'), may hold values from -5.5 to 5.5
- pre_key: bfloat16 [4096, 3072], P('req', 'head'), may hold values from -6 to 6
- pre_value: bfloat16 [4096, 3072], P('req', 'head'), may hold values from -6 to 6
- cache_key: bfloat16 [32, 2048, 3072], P('req', None, 'head'), may hold values from -5.5 to 5.5
- cache_value: bfloat16 [32, 2048, 3072], P('req', None, 'head'), may hold values from -6 to 6
- group_of: int32 [768, 1], replicated, may hold values from 0 to 31; in each aligned block of 768 rows (0 to 767, 768 to 1535, ...) at most 48 rows name the same one
- cache_length: int32 [32], P('req'), may hold values from 256 to 2048, as said below
- stretch_start: int32 [16], P('req'), may hold values from 256 to 2048, as said below
- row_owner: int32 [4864, 1], P('req'), may hold values from 0 to 15; in each aligned block of 304 rows (0 to 303, 304 to 607, ...) at most 40 rows name the same one
- out_weight: bfloat16 [3072, 3072], P('head'), may hold values from -0.109375 to 0.109375
- norm_gain: float32 [3072], replicated, may hold values from 0.1 to 1.9
- gate_weight: bfloat16 [3072, 4096], P(None, 'head'), may hold values from -0.109375 to 0.109375
- up_weight: bfloat16 [3072, 4096], P(None, 'head'), may hold values from -0.109375 to 0.109375
- down_weight: bfloat16 [4096, 3072], P('head'), may hold values from -0.09375 to 0.09375
Outputs:
- layer_out: bfloat16 [10240, 3072], P(('req', 'head'))
Inputs may be any that keep to these rules, and one draw needn't show every extreme that they name: `group_of`: at most 48 requests share a cache group, exactly 48 in some group; every group has a request. `cache_length`: some group has all 2048 rows valid. `stretch_start`: some stretch follows all 2048 cached rows. `row_owner`: among the 304 rows of one index of req at most 40 share an owner, exactly 40 on some index.
All inputs are finite; a program needn't handle non-finite values.
Results may differ from a plain program's by a relative error of at most 0.02.
Values may be sent and summed in bfloat16 or wider, within the bound.
No kernel may reach another device: no remote copies, remote signals or barrier semaphores. Data moves between devices by JAX's collectives and lax.ppermute only.
A program may use at most 128 MiB of HBM per device.

v0:
```python
import math
import jax
import jax.numpy as jnp
from jax import lax
from jax.sharding import PartitionSpec as P

HD = 96
CAP = 48
eps_norm = 1e-05


def head_split(matrix):
    return matrix.reshape(matrix.shape[0], matrix.shape[1] // HD, HD)


def softmax_rows(scores, allowed):
    masked = jnp.where(allowed, scores, -jnp.inf)
    highest = jnp.max(masked, axis=-1, keepdims=True)
    raised = jnp.exp(masked - highest)
    return (raised / jnp.sum(raised, axis=-1, keepdims=True)).astype(jnp.bfloat16)


def on_device(
    hidden_in,
    dec_query,
    dec_key,
    dec_value,
    pre_query,
    pre_key,
    pre_value,
    cache_key,
    cache_value,
    group_of,
    cache_length,
    stretch_start,
    row_owner,
    out_weight,
    norm_gain,
    gate_weight,
    up_weight,
    down_weight,
):
    factor = 1.0 / math.sqrt(HD)
    width_here = dec_query.shape[1]
    queries_all, keys_own, values_own = (
        lax.all_gather(dec_query, "req", axis=0, tiled=True),
        lax.all_gather(dec_key, "req", axis=0, tiled=True),
        lax.all_gather(dec_value, "req", axis=0, tiled=True),
    )
    groups_here = cache_key.shape[0]
    length_cache = cache_key.shape[1]
    first_group = lax.axis_index("req") * groups_here
    members = group_of[:, 0]
    wanted = first_group + jnp.arange(groups_here, dtype=jnp.int32)
    belongs = (members[None, :] == wanted[:, None]).astype(jnp.int32)
    ranking = jnp.cumsum(belongs, axis=1) - 1
    places = jnp.arange(CAP, dtype=jnp.int32)
    chosen = (belongs[:, None, :] == 1) & (ranking[:, None, :] == places[None, :, None])
    chooser = chosen.reshape(groups_here * CAP, members.shape[0])
    stacked_in = jnp.concatenate([queries_all, keys_own, values_own], axis=1)
    picked = jnp.dot(
        chooser.astype(jnp.bfloat16), stacked_in, preferred_element_type=jnp.float32
    ).astype(jnp.bfloat16)
    positions = jnp.arange(length_cache)
    results = []
    for group_pos in range(groups_here):
        rows_block = picked[group_pos * CAP : (group_pos + 1) * CAP]
        picked_q = head_split(rows_block[:, :width_here])
        picked_k = head_split(rows_block[:, width_here : 2 * width_here])
        picked_v = head_split(rows_block[:, 2 * width_here :])
        cache_scores = (
            jnp.einsum(
                "qhd,khd->hqk",
                picked_q,
                head_split(cache_key[group_pos]),
                preferred_element_type=jnp.float32,
            )
            * factor
        )
        own_scores = (
            jnp.sum(picked_q.astype(jnp.float32) * picked_k.astype(jnp.float32), axis=-1).T * factor
        )
        scores = jnp.concatenate([cache_scores, own_scores[:, :, None]], axis=-1)
        allowed = jnp.concatenate([positions < cache_length[group_pos], jnp.ones((1,), bool)])[
            None, None, :
        ]
        weights = softmax_rows(scores, allowed)
        blended = jnp.einsum(
            "hqk,khd->qhd",
            weights[:, :, :length_cache],
            head_split(cache_value[group_pos]),
            preferred_element_type=jnp.float32,
        )
        blended = blended + weights[:, :, length_cache].astype(jnp.float32).T[
            :, :, None
        ] * picked_v.astype(jnp.float32)
        results.append(blended.reshape(CAP, width_here))
    stacked = jnp.concatenate(results, axis=0)
    spread_back = jnp.dot(chooser.astype(jnp.float32).T, stacked, precision=lax.Precision.HIGHEST)
    dec_out = lax.psum_scatter(
        spread_back.astype(jnp.bfloat16), "req", scatter_dimension=0, tiled=True
    )
    stretch_len = pre_query.shape[0]
    key_rows = jnp.concatenate([cache_key[0], pre_key], axis=0)
    value_rows = jnp.concatenate([cache_value[0], pre_value], axis=0)
    columns = jnp.arange(length_cache + stretch_len)
    row_numbers = jnp.arange(stretch_len)
    allowed_pre = jnp.where(
        columns[None, :] < length_cache,
        columns[None, :] < stretch_start[0],
        columns[None, :] - length_cache <= row_numbers[:, None],
    )
    pre_scores = (
        jnp.einsum(
            "qhd,khd->hqk",
            head_split(pre_query),
            head_split(key_rows),
            preferred_element_type=jnp.float32,
        )
        * factor
    )
    pre_weights = softmax_rows(pre_scores, allowed_pre[None])
    pre_mixed = jnp.einsum(
        "hqk,khd->qhd", pre_weights, head_split(value_rows), preferred_element_type=jnp.float32
    )
    pre_out = pre_mixed.reshape(stretch_len, width_here).astype(jnp.bfloat16)
    attn_rows = jnp.concatenate([dec_out, pre_out], axis=0)
    projected = jnp.dot(attn_rows, out_weight, preferred_element_type=jnp.float32)
    col_start = lax.axis_index("head") * width_here
    own_cols = lax.dynamic_slice_in_dim(projected, col_start, width_here, 1) + hidden_in.astype(
        jnp.float32
    )
    contribution = lax.dynamic_update_slice_in_dim(projected, own_cols, col_start, 1)
    req_count = lax.axis_size("req")
    row_count = contribution.shape[0]
    slot_rows = 8 * ((2 * row_count + 8 * req_count - 1) // (8 * req_count))
    owners = row_owner[:, 0]
    onehot_owner = (owners[:, None] == jnp.arange(req_count, dtype=jnp.int32)[None, :]).astype(
        jnp.int32
    )
    before = jnp.sum((jnp.cumsum(onehot_owner, axis=0) - 1) * onehot_owner, axis=1)
    target = owners * slot_rows + before
    placing = (
        target[None, :] == jnp.arange(req_count * slot_rows, dtype=jnp.int32)[:, None]
    ).astype(jnp.bfloat16)
    residual = lax.psum(contribution.astype(jnp.bfloat16), "head")
    outgoing = jnp.dot(placing, residual, preferred_element_type=jnp.float32).astype(jnp.bfloat16)
    arrived = lax.all_to_all(outgoing, "req", split_axis=0, concat_axis=0, tiled=True)
    arrived_wide = arrived.astype(jnp.float32)
    squares = jnp.mean(jnp.square(arrived_wide), axis=-1, keepdims=True)
    normed = (arrived_wide * lax.rsqrt(squares + eps_norm) * norm_gain).astype(jnp.bfloat16)
    gate_act = jnp.dot(normed, gate_weight, preferred_element_type=jnp.float32)
    up_act = jnp.dot(normed, up_weight, preferred_element_type=jnp.float32)
    hidden = (jax.nn.silu(gate_act) * up_act).astype(jnp.bfloat16)
    rows_here = arrived.shape[0] // lax.axis_size("head")
    down_sum = lax.psum_scatter(
        jnp.dot(hidden, down_weight, preferred_element_type=jnp.float32).astype(jnp.bfloat16),
        "head",
        scatter_dimension=0,
        tiled=True,
    ).astype(jnp.float32)
    own_rows = lax.dynamic_slice_in_dim(
        arrived_wide, lax.axis_index("head") * rows_here, rows_here, 0
    )
    return (own_rows + down_sum).astype(jnp.bfloat16)


def solution(mesh):
    placed = (
        P("req", "head"),
        P("req", "head"),
        P("req", "head"),
        P("req", "head"),
        P("req", "head"),
        P("req", "head"),
        P("req", "head"),
        P("req", None, "head"),
        P("req", None, "head"),
        P(),
        P("req"),
        P("req"),
        P("req", None),
        P("head", None),
        P(),
        P(None, "head"),
        P(None, "head"),
        P("head", None),
    )
    return jax.shard_map(
        on_device, mesh=mesh, in_specs=placed, out_specs=P(("req", "head"), None), check_vma=False
    )
```

profile of v0, /device:TPU:0, one launch (start us, length us, event | category | flops | bytes accessed | tf_op | source)
XLA Modules:
  0.0 390.3 jit_solution(7005297331430344854)
XLA Ops:
  11.9 24.6 %all_gather.9 = bf16[768,384]{1,0:T(8,128)(2,1)S(1)} all-gather(bf16[48,384]{1,0:T(8,128)(2,1)} %param.19), channel_id=1, replica_groups=mesh['req'=16,'head'=8] {'req'}, dimensions={0}, use_global_device_ids=true | all-gather | bytes 626688 | tf_op jit(solution)/shard_map/all_gather | solution.py:46
  36.5 23.5 %all_gather.10 = bf16[768,384]{1,0:T(8,128)(2,1)S(1)} all-gather(bf16[48,384]{1,0:T(8,128)(2,1)} %param.20), channel_id=1, replica_groups=mesh['req'=16,'head'=8] {'req'}, dimensions={0}, use_global_device_ids=true | all-gather | bytes 626688 | tf_op jit(solution)/shard_map/all_gather | solution.py:47
  60.0 21.9 %all_gather.11 = bf16[768,384]{1,0:T(8,128)(2,1)S(1)} all-gather(bf16[48,384]{1,0:T(8,128)(2,1)} %param.21), channel_id=1, replica_groups=mesh['req'=16,'head'=8] {'req'}, dimensions={0}, use_global_device_ids=true | all-gather | bytes 626688 | tf_op jit(solution)/shard_map/all_gather | solution.py:48
  89.7 3.9 fusion.81
  93.5 2.6 copy.77
  99.7 2.6 copy.70
  108.2 2.6 copy.81
  110.8 2.3 fusion.31
  113.3 2.7 copy.74
  115.9 2.3 fusion.32
  125.4 3.8 fusion.12
  129.2 4.9 %fusion.84 = f32[4,256]{1,0:T(4,128)S(1)} fusion(pred[256,2304]{0,1:T(8,128)(4,1)} %fusion.12, bf16[256,4,96]{0,2,1:T(8,128)(2,1)S(1)} %bitcast.97, bf16[256,4,96]{0,2,1:T(8,128)(2,1)S(1)} %bitcast.99, bf16[2048,4,96]{0,2,1:T(8,128)(2,1)} %bitcast.90), kind=kOutput, calls=%fused_computation.125 | convolution fusion | flops 465963264 | bytes 2560000 | tf_op jit(solution)/shard_map/sub | solution.py:19
  134.0 7.6 %fusion.28 = bf16[4,96,256]{2,1,0:T(8,128)(2,1)} fusion(f32[4,256]{1,0:T(4,128)S(1)} %fusion.84, bf16[256,4,96]{0,2,1:T(8,128)(2,1)} %bitcast.101, bf16[2048,4,96]{0,2,1:T(8,128)(2,1)} %bitcast.93, pred[256,2304]{0,1:T(8,128)(4,1)} %fusion.12, bf16[256,4,96]{0,2,1:T(8,128)(2,1)S(1)} %bitcast.98, bf16[256,4,96]{0,2,1:T(8,128)(2,1)S(1)} %bitcast.100, ...), kind=kOutput, calls=%fused_computation.45 | convolution fusion | flops 924945664 | bytes 4526080 | tf_op jit(solution)/shard_map/hqk,khd->qhd/dot_general | solution.py:123
  141.7 51.4 %reduce-scatter.7.cloned.1.call-done = bf16[48,384]{1,0:T(8,128)(2,1)} async-done(((bf16[768,384]{1,0:T(8,128)(2,1)}), bf16[48,384]{1,0:T(8,128)(2,1)}) %reduce-scatter.7.cloned.1.call-update) | async-done | bytes 36880
  193.9 3.1 fusion.44
  200.2 63.4 %all-reduce.4.cloned.1.call-done = bf16[304,3072]{1,0:T(8,128)(2,1)} async-done(((bf16[304,3072]{1,0:T(8,128)(2,1)}), bf16[304,3072]{1,0:T(8,128)(2,1)}) %all-reduce.4.cloned.1.call-update) | async-done | bytes 1867792 | tf_op jit(solution)/shard_map/psum | solution.py:146
  263.6 3.7 convolution_convert_fusion.1
  267.3 52.8 %all_to_all.9 = bf16[16,40,3072]{2,1,0:T(8,128)(2,1)S(1)} all-to-all(bf16[16,40,3072]{2,1,0:T(8,128)(2,1)S(1)} %bitcast.96), channel_id=1, replica_groups=mesh['req'=16,'head'=8] {'req'}, dimensions={0} | all-to-all | bytes 7864320 | tf_op jit(solution)/shard_map/all_to_all | solution.py:148
  322.2 6.9 %multiply_convert_fusion = (bf16[640,3072]{1,0:T(8,128)(2,1)S(1)}, f32[16,40,3072]{2,1,0:T(8,128)}) fusion(f32[3072]{0:T(1024)S(1)} %copy-done.10, f32[640]{0:T(1024)S(1)} %rsqrt.12, bf16[16,40,3072]{2,1,0:T(8,128)(2,1)} %copy-done.1), kind=kLoop, calls=%fused_computation.7 | loop fusion | flops 7864320 | bytes 15743488 | tf_op jit(solution)/shard_map/convert_element_type | solution.py:151
  329.1 2.0 copy-done.2
  331.1 3.2 fusion.89
  334.4 9.7 %convolution_convert_fusion = bf16[640,3072]{1,0:T(8,128)(2,1)} fusion(bf16[512,3072]{1,0:T(8,128)(2,1)S(1)} %copy-done, bf16[640,3072]{1,0:T(8,128)(2,1)} %copy-done.2, bf16[3072,512]{1,0:T(8,128)(2,1)} %param.34, f32[640,512]{1,0:T(8,128)} %fusion.89), kind=kOutput, calls=%fused_computation.9 | convolution fusion | flops 4030464000 | bytes 15466496 | tf_op jit(solution)/shard_map/dot_general | solution.py:157
  344.1 37.5 %reduce-scatter.5.cloned.1.call-done = bf16[80,3072]{1,0:T(8,128)(2,1)} async-done(((bf16[640,3072]{1,0:T(8,128)(2,1)}), bf16[80,3072]{1,0:T(8,128)(2,1)}) %reduce-scatter.5.cloned.1.call-update) | async-done | bytes 491536 | tf_op jit(solution)/shard_map/reduce_scatter | solution.py:156
  381.6 2.2 add_convert_fusion
  (97 shorter events, 35.0 us)
Async XLA Ops:
  6.5 327.8 %copy-start = (bf16[512,3072]{1,0:T(8,128)(2,1)S(1)}, bf16[512,3072]{1,0:T(8,128)(2,1)}, u32[]{:S(2)}) copy-start(bf16[512,3072]{1,0:T(8,128)(2,1)} %param.35) | copy-start | bytes 9437188
  6.5 186.5 %reduce-scatter.7.cloned.1.call-start = ((), (), s32[]{:S(2)}) async-start(), calls=%async_computation.5 | async-start | bytes 626688
  82.1 0.6 copy-start.6
  96.2 1.8 copy-start.11
  96.2 1.8 copy-start.9
  98.7 0.9 copy-start.3
  104.0 2.2 copy-start.5
  104.7 0.9 copy-start.4
  115.9 2.5 copy-start.7
  115.9 4.9 %copy-start.12 = (s32[304,1]{0,1:T(1,128)S(1)}, s32[304,1]{0,1:T(1,128)}, u32[]{:S(2)}) copy-start(s32[304,1]{0,1:T(1,128)} %param.30) | copy-start | bytes 3652
  120.0 143.6 %all-reduce.4.cloned.1.call-start = ((), (), s32[]{:S(2)}) async-start(), calls=%async_computation.3 | async-start | bytes 3735552 | tf_op jit(solution)/shard_map/psum | solution.py:146
  193.9 3.1 copy-start.8
  198.6 182.9 %reduce-scatter.5.cloned.1.call-start = ((), (), s32[]{:S(2)}) async-start(), calls=%async_computation.4 | async-start | bytes 4423680 | tf_op jit(solution)/shard_map/reduce_scatter | solution.py:156
  320.1 2.0 copy-start.1
  320.1 2.1 copy-start.10
  322.2 8.9 %copy-start.13 = (bf16[3072,512]{1,0:T(8,128)(2,1)S(1)}, bf16[3072,512]{1,0:T(8,128)(2,1)}, u32[]{:S(2)}) copy-start(bf16[3072,512]{1,0:T(8,128)(2,1)} %param.33) | copy-start | bytes 9437188
  329.1 2.0 copy-start.2
Sparse Core Ops, SparseCore 0:
  120.1 72.9 reduce-scatter.6
  198.8 64.7 all-reduce.3
  344.2 37.3 reduce-scatter.4
where the time goes:
time: 392 us; the launch traced here: 390 us
  waiting for transfers between devices  152 us (39%)
  blocking collectives  123 us (31%)
  matrix products  42.3 us (11%)
  local copies, waits for them, and re-layouts  34.5 us (9%)
  other arithmetic  23.7 us (6%)
  between operations  14.1 us (4%)
    psum x1, waiting for transfers between devices, on_device(): residual = lax.psum(contribution.astype(jnp.bfloat16), 'head')  63.4 us
    all_to_all x1, blocking collectives, on_device(): lax.all_to_all(outgoing, 'req', split_axis=0, concat_axis=0, tiled=True)  52.8 us
    unnamed x4, waiting for transfers between devices  51.4 us
    reduce_scatter x1, waiting for transfers between devices, on_device(): lax.psum_scatter(jnp.dot(hidden, down_weight, preferred_element_type=jnp....  37.5 us
    all_gather x1, blocking collectives, on_device(): lax.all_gather(dec_query, 'req', axis=0, tiled=True)  24.6 us
    all_gather x1, blocking collectives, on_device(): lax.all_gather(dec_key, 'req', axis=0, tiled=True)  23.5 us
    all_gather x1, blocking collectives, on_device(): lax.all_gather(dec_value, 'req', axis=0, tiled=True)  21.9 us
    dot_general x1, matrix products, on_device(): jnp.dot(hidden, down_weight, preferred_element_type=jnp.float32)  9.69 us
  transfers between devices with their start and end apart: 3, of which 3 were waited for; matrix products, arithmetic and copies ran while one was open for 6% of the time, Pallas kernels for 0%

commit v1 on v0

--- a/solution.py
+++ b/solution.py
@@ -7,6 +7,22 @@
 HD = 96
 CAP = 48
 eps_norm = 1e-05
+
+
+def collect(x, axis, dim):
+    ways, here, step = (lax.axis_size(axis), lax.axis_index(axis), x.shape[dim])
+    shape = [n * ways if d == dim else n for d, n in enumerate(x.shape)]
+    full = lax.dynamic_update_slice_in_dim(jnp.zeros(shape, x.dtype), x, here * step, axis=dim)
+    going_up = going_down = x
+    for far in range(1, ways // 2 + 1):
+        going_up = lax.ppermute(going_up, axis, [(d, (d + 1) % ways) for d in range(ways)])
+        full = lax.dynamic_update_slice_in_dim(full, going_up, (here - far) % ways * step, axis=dim)
+        if 2 * far < ways:
+            going_down = lax.ppermute(going_down, axis, [(d, (d - 1) % ways) for d in range(ways)])
+            full = lax.dynamic_update_slice_in_dim(
+                full, going_down, (here + far) % ways * step, axis=dim
+            )
+    return full
 
 
 def head_split(matrix):
@@ -43,7 +59,7 @@
     factor = 1.0 / math.sqrt(HD)
     width_here = dec_query.shape[1]
     queries_all, keys_own, values_own = (
-        lax.all_gather(dec_query, "req", axis=0, tiled=True),
+        collect(dec_query, "req", 0),
         lax.all_gather(dec_key, "req", axis=0, tiled=True),
         lax.all_gather(dec_value, "req", axis=0, tiled=True),
     )

time: 392 us -> 440 us (1.12)
  starting transfers between devices: 0.49 us -> 36.3 us
  blocking collectives: 123 us -> 105 us
  waiting for transfers between devices: 152 us -> 169 us
  local copies, waits for them, and re-layouts: 34.5 us -> 48.3 us
    ppermute x0 -> x15, starting transfers between devices: none -> 36 us  [the longest x7 36 us: collect(): lax.ppermute(going_down, axis, [(d, (d - 1) % ways) for d in range(ways)])]
    all_gather x1 -> x0, blocking collectives: 24.6 us -> none  [on_device(): lax.all_gather(dec_query, 'req', axis=0, tiled=True)]
    ppermute x0 -> x15, waiting for transfers between devices: none -> 13.7 us  [the longest x8 12.1 us: collect(): lax.ppermute(going_up, axis, [(d, (d + 1) % ways) for d in range(ways)])]
    dynamic_update_slice x0 -> x16, local copies, waits for them, and re-layouts: none -> 12.1 us  [the longest x8 5.7 us: collect(): lax.dynamic_update_slice_in_dim(full, going_up, (here - far) % ways * ste...]
    unnamed x32 -> x52, local copies, waits for them, and re-layouts: 9.55 us -> 9.68 us
  transfers between devices with their start and end apart: 3 -> 18, of which waited for: 3 -> 9; matrix products, arithmetic and copies ran while one was open for 6% -> 13% of each run, Pallas kernels for 0% -> 0%
where the time goes in v1:
time: 440 us; the launch traced here: 439 us
  waiting for transfers between devices  169 us (38%)
  blocking collectives  105 us (24%)
  local copies, waits for them, and re-layouts  48.3 us (11%)
  matrix products  40.8 us (9%)
  starting transfers between devices  36.3 us (8%)
  other arithmetic  25.3 us (6%)
  between operations  14.2 us (3%)
    psum x1, waiting for transfers between devices, on_device(): residual = lax.psum(contribution.astype(jnp.bfloat16), 'head')  63.3 us
    unnamed x4, waiting for transfers between devices  54.9 us
    all_to_all x1, blocking collectives, on_device(): lax.all_to_all(outgoing, 'req', split_axis=0, concat_axis=0, tiled=True)  52.8 us
    reduce_scatter x1, waiting for transfers between devices, on_device(): lax.psum_scatter(jnp.dot(hidden, down_weight, preferred_element_type=jnp....  37.5 us
    ppermute x7, starting transfers between devices, collect(): lax.ppermute(going_down, axis, [(d, (d - 1) % ways) for d in range(ways)])  36 us
    all_gather x1, blocking collectives, on_device(): lax.all_gather(dec_key, 'req', axis=0, tiled=True)  27.1 us
    all_gather x1, blocking collectives, on_device(): lax.all_gather(dec_value, 'req', axis=0, tiled=True)  24.8 us
    ppermute x8, waiting for transfers between devices, collect(): lax.ppermute(going_up, axis, [(d, (d + 1) % ways) for d in range(ways)])  12.1 us
  transfers between devices with their start and end apart: 18, of which 9 were waited for; matrix products, arithmetic and copies ran while one was open for 13% of the time, Pallas kernels for 0%

profile of v1, /device:TPU:0, one launch (start us, length us, event | category | flops | bytes accessed | tf_op | source)
XLA Modules:
  0.0 439.1 jit_solution(12094074091192103739)
XLA Ops:
  6.5 5.3 %collective-permute-start.1 = (bf16[48,384]{1,0:T(8,128)(2,1)}, bf16[48,384]{1,0:T(8,128)(2,1)}, u32[]{:S(2)}, u32[]{:S(2)}) collective-permute-start(bf16[48,384]{1,0:T(8,128)(2,1)} %param.19), channel_id=1, source_target_pairs={{0,120},{8,0},{16,8},{24,16},{32,24},{40,32},{48,40},{56,48},{64,5... | collective-permute-start | bytes 110600 | tf_op jit(solution)/shard_map/ppermute | solution.py:21
  19.0 27.1 %all_gather.6 = bf16[768,384]{1,0:T(8,128)(2,1)} all-gather(bf16[48,384]{1,0:T(8,128)(2,1)} %param.20), channel_id=1, replica_groups=mesh['req'=16,'head'=8] {'req'}, dimensions={0}, use_global_device_ids=true | all-gather | bytes 626688 | tf_op jit(solution)/shard_map/all_gather | solution.py:63
  46.0 24.8 %all_gather.7 = bf16[768,384]{1,0:T(8,128)(2,1)} all-gather(bf16[48,384]{1,0:T(8,128)(2,1)} %param.21), channel_id=1, replica_groups=mesh['req'=16,'head'=8] {'req'}, dimensions={0}, use_global_device_ids=true | all-gather | bytes 626688 | tf_op jit(solution)/shard_map/all_gather | solution.py:64
  70.9 4.0 fusion.81
  96.4 2.7 collective-permute-start.3
  101.9 5.3 %collective-permute-start.5 = (bf16[48,384]{1,0:T(8,128)(2,1)S(1)}, bf16[48,384]{1,0:T(8,128)(2,1)S(1)}, u32[]{:S(2)}, u32[]{:S(2)}) collective-permute-start(bf16[48,384]{1,0:T(8,128)(2,1)S(1)} %collective-permute-done.3), channel_id=1, source_target_pairs={{0,120},{8,0},{16,8},{24,16},{32,24},{40,32},{48,40},{56,48},{64,5... | collective-permute-start | bytes 110600 | tf_op jit(solution)/shard_map/ppermute | solution.py:21
  108.9 5.7 %collective-permute-start.7 = (bf16[48,384]{1,0:T(8,128)(2,1)S(1)}, bf16[48,384]{1,0:T(8,128)(2,1)S(1)}, u32[]{:S(2)}, u32[]{:S(2)}) collective-permute-start(bf16[48,384]{1,0:T(8,128)(2,1)S(1)} %collective-permute-done.5), channel_id=1, source_target_pairs={{0,120},{8,0},{16,8},{24,16},{32,24},{40,32},{48,40},{56,48},{64,5... | collective-permute-start | bytes 110600 | tf_op jit(solution)/shard_map/ppermute | solution.py:21
  116.2 5.6 %collective-permute-start.9 = (bf16[48,384]{1,0:T(8,128)(2,1)S(1)}, bf16[48,384]{1,0:T(8,128)(2,1)S(1)}, u32[]{:S(2)}, u32[]{:S(2)}) collective-permute-start(bf16[48,384]{1,0:T(8,128)(2,1)S(1)} %collective-permute-done.7), channel_id=1, source_target_pairs={{0,120},{8,0},{16,8},{24,16},{32,24},{40,32},{48,40},{56,48},{64,5... | collective-permute-start | bytes 110600 | tf_op jit(solution)/shard_map/ppermute | solution.py:21
  123.5 5.6 %collective-permute-start.11 = (bf16[48,384]{1,0:T(8,128)(2,1)S(1)}, bf16[48,384]{1,0:T(8,128)(2,1)S(1)}, u32[]{:S(2)}, u32[]{:S(2)}) collective-permute-start(bf16[48,384]{1,0:T(8,128)(2,1)S(1)} %collective-permute-done.9), channel_id=1, source_target_pairs={{0,120},{8,0},{16,8},{24,16},{32,24},{40,32},{48,40},{56,48},{64,5... | collective-permute-start | bytes 110600 | tf_op jit(solution)/shard_map/ppermute | solution.py:21
  130.8 5.6 %collective-permute-start.13 = (bf16[48,384]{1,0:T(8,128)(2,1)S(1)}, bf16[48,384]{1,0:T(8,128)(2,1)S(1)}, u32[]{:S(2)}, u32[]{:S(2)}) collective-permute-start(bf16[48,384]{1,0:T(8,128)(2,1)S(1)} %collective-permute-done.11), channel_id=1, source_target_pairs={{0,120},{8,0},{16,8},{24,16},{32,24},{40,32},{48,40},{56,48},{64,5... | collective-permute-start | bytes 110600 | tf_op jit(solution)/shard_map/ppermute | solution.py:21
  137.7 6.0 %collective-permute-done.12 = bf16[48,384]{1,0:T(8,128)(2,1)S(1)} collective-permute-done((bf16[48,384]{1,0:T(8,128)(2,1)S(1)}, bf16[48,384]{1,0:T(8,128)(2,1)S(1)}, u32[]{:S(2)}, u32[]{:S(2)}) %collective-permute-start.12) | collective-permute-done | bytes 36896 | tf_op jit(solution)/shard_map/ppermute | solution.py:18
  144.9 6.0 %collective-permute-done.14 = bf16[48,384]{1,0:T(8,128)(2,1)S(1)} collective-permute-done((bf16[48,384]{1,0:T(8,128)(2,1)S(1)}, bf16[48,384]{1,0:T(8,128)(2,1)S(1)}, u32[]{:S(2)}, u32[]{:S(2)}) %collective-permute-start.14) | collective-permute-done | bytes 36896 | tf_op jit(solution)/shard_map/ppermute | solution.py:18
  171.7 2.7 fusion.12
  174.4 5.0 %fusion.84 = f32[4,256]{1,0:T(4,128)S(1)} fusion(pred[256,2304]{0,1:T(8,128)(4,1)} %fusion.12, bf16[256,4,96]{0,2,1:T(8,128)(2,1)} %bitcast.97, bf16[256,4,96]{0,2,1:T(8,128)(2,1)} %bitcast.99, bf16[2048,4,96]{0,2,1:T(8,128)(2,1)} %bitcast.89), kind=kOutput, calls=%fused_computation.141 | convolution fusion | flops 465963264 | bytes 2560000 | tf_op jit(solution)/shard_map/sub | solution.py:35
  179.5 7.6 %fusion.28 = bf16[4,96,256]{2,1,0:T(8,128)(2,1)} fusion(f32[4,256]{1,0:T(4,128)S(1)} %fusion.84, bf16[256,4,96]{0,2,1:T(8,128)(2,1)} %bitcast.101, bf16[2048,4,96]{0,2,1:T(8,128)(2,1)} %bitcast.93, pred[256,2304]{0,1:T(8,128)(4,1)} %fusion.12, bf16[256,4,96]{0,2,1:T(8,128)(2,1)S(1)} %bitcast.98, bf16[256,4,96]{0,2,1:T(8,128)(2,1)S(1)} %bitcast.100, ...), kind=kOutput, calls=%fused_computation.45 | convolution fusion | flops 924945664 | bytes 4526080 | tf_op jit(solution)/shard_map/hqk,khd->qhd/dot_general | solution.py:139
  187.0 54.9 %reduce-scatter.7.cloned.1.call-done = bf16[48,384]{1,0:T(8,128)(2,1)} async-done(((bf16[768,384]{1,0:T(8,128)(2,1)}), bf16[48,384]{1,0:T(8,128)(2,1)}) %reduce-scatter.7.cloned.1.call-update) | async-done | bytes 36880
  242.8 3.1 fusion.44
  249.1 63.3 %all-reduce.4.cloned.1.call-done = bf16[304,3072]{1,0:T(8,128)(2,1)} async-done(((bf16[304,3072]{1,0:T(8,128)(2,1)}), bf16[304,3072]{1,0:T(8,128)(2,1)}) %all-reduce.4.cloned.1.call-update) | async-done | bytes 1867792 | tf_op jit(solution)/shard_map/psum | solution.py:162
  312.4 3.7 convolution_convert_fusion.1
  316.1 52.8 %all_to_all.9 = bf16[16,40,3072]{2,1,0:T(8,128)(2,1)S(1)} all-to-all(bf16[16,40,3072]{2,1,0:T(8,128)(2,1)S(1)} %bitcast.96), channel_id=1, replica_groups=mesh['req'=16,'head'=8] {'req'}, dimensions={0} | all-to-all | bytes 7864320 | tf_op jit(solution)/shard_map/all_to_all | solution.py:164
  371.0 6.9 %multiply_convert_fusion = (bf16[640,3072]{1,0:T(8,128)(2,1)S(1)}, f32[16,40,3072]{2,1,0:T(8,128)}) fusion(f32[3072]{0:T(1024)S(1)} %copy-done.17, f32[640]{0:T(1024)S(1)} %rsqrt.12, bf16[16,40,3072]{2,1,0:T(8,128)(2,1)} %copy-done.1), kind=kLoop, calls=%fused_computation.7 | loop fusion | flops 7864320 | bytes 15743488 | tf_op jit(solution)/shard_map/convert_element_type | solution.py:167
  379.9 3.2 fusion.89
  383.2 9.7 %convolution_convert_fusion = bf16[640,3072]{1,0:T(8,128)(2,1)} fusion(bf16[512,3072]{1,0:T(8,128)(2,1)S(1)} %copy-done, bf16[640,3072]{1,0:T(8,128)(2,1)} %copy-done.4, bf16[3072,512]{1,0:T(8,128)(2,1)} %param.34, f32[640,512]{1,0:T(8,128)} %fusion.89), kind=kOutput, calls=%fused_computation.9 | convolution fusion | flops 4030464000 | bytes 15466496 | tf_op jit(solution)/shard_map/dot_general | solution.py:173
  392.9 37.5 %reduce-scatter.5.cloned.1.call-done = bf16[80,3072]{1,0:T(8,128)(2,1)} async-done(((bf16[640,3072]{1,0:T(8,128)(2,1)}), bf16[80,3072]{1,0:T(8,128)(2,1)}) %reduce-scatter.5.cloned.1.call-update) | async-done | bytes 491536 | tf_op jit(solution)/shard_map/reduce_scatter | solution.py:172
  (163 shorter events, 70.4 us)
Async XLA Ops:
  6.5 376.6 %copy-start = (bf16[512,3072]{1,0:T(8,128)(2,1)S(1)}, bf16[512,3072]{1,0:T(8,128)(2,1)}, u32[]{:S(2)}) copy-start(bf16[512,3072]{1,0:T(8,128)(2,1)} %param.35) | copy-start | bytes 9437188
  6.5 235.4 %reduce-scatter.7.cloned.1.call-start = ((), (), s32[]{:S(2)}) async-start(), calls=%async_computation.5 | async-start | bytes 626688
  6.5 89.9 %collective-permute-start.1 = (bf16[48,384]{1,0:T(8,128)(2,1)}, bf16[48,384]{1,0:T(8,128)(2,1)}, u32[]{:S(2)}, u32[]{:S(2)}) collective-permute-start(bf16[48,384]{1,0:T(8,128)(2,1)} %param.19), channel_id=1, source_target_pairs={{0,120},{8,0},{16,8},{24,16},{32,24},{40,32},{48,40},{56,48},{64,5... | collective-permute-start | bytes 110600 | tf_op jit(solution)/shard_map/ppermute | solution.py:21
  11.9 87.3 %collective-permute-start = (bf16[48,384]{1,0:T(8,128)(2,1)}, bf16[48,384]{1,0:T(8,128)(2,1)}, u32[]{:S(2)}, u32[]{:S(2)}) collective-permute-start(bf16[48,384]{1,0:T(8,128)(2,1)} %param.19), channel_id=1, source_target_pairs={{0,8},{8,16},{16,24},{24,32},{32,40},{40,48},{48,56},{56,64},{64,7... | collective-permute-start | bytes 110600 | tf_op jit(solution)/shard_map/ppermute | solution.py:18
  74.9 7.5 %copy-start.10 = (bf16[256,384]{1,0:T(8,128)(2,1)S(1)}, bf16[256,384]{1,0:T(8,128)(2,1)}, u32[]{:S(2)}) copy-start(bf16[256,384]{1,0:T(8,128)(2,1)} %param.22) | copy-start | bytes 589828
  74.9 8.3 %copy-start.11 = (bf16[256,384]{1,0:T(8,128)(2,1)S(1)}, bf16[256,384]{1,0:T(8,128)(2,1)}, u32[]{:S(2)}) copy-start(bf16[256,384]{1,0:T(8,128)(2,1)} %param.23) | copy-start | bytes 589828
  96.4 57.1 %copy-start.7 = (pred[96,768]{1,0:T(32,128)(4,1)}, pred[96,768]{1,0:T(32,128)(4,1)S(1)}, u32[]{:S(2)}) copy-start(pred[96,768]{1,0:T(32,128)(4,1)S(1)} %fusion.48) | copy-start | bytes 221188
  96.4 5.5 %collective-permute-start.3 = (bf16[48,384]{1,0:T(8,128)(2,1)}, bf16[48,384]{1,0:T(8,128)(2,1)S(1)}, u32[]{:S(2)}, u32[]{:S(2)}) collective-permute-start(bf16[48,384]{1,0:T(8,128)(2,1)} %collective-permute-done.1), channel_id=1, source_target_pairs={{0,120},{8,0},{16,8},{24,16},{32,24},{40,32},{48,40},{56,48},{64,5... | collective-permute-start | bytes 110600 | tf_op jit(solution)/shard_map/ppermute | solution.py:21
  99.1 8.1 %collective-permute-start.2 = (bf16[48,384]{1,0:T(8,128)(2,1)}, bf16[48,384]{1,0:T(8,128)(2,1)S(1)}, u32[]{:S(2)}, u32[]{:S(2)}) collective-permute-start(bf16[48,384]{1,0:T(8,128)(2,1)} %collective-permute-done), channel_id=1, source_target_pairs={{0,8},{8,16},{16,24},{24,32},{32,40},{40,48},{48,56},{56,64},{64,7... | collective-permute-start | bytes 110600 | tf_op jit(solution)/shard_map/ppermute | solution.py:18
  101.9 7.0 %collective-permute-start.5 = (bf16[48,384]{1,0:T(8,128)(2,1)S(1)}, bf16[48,384]{1,0:T(8,128)(2,1)S(1)}, u32[]{:S(2)}, u32[]{:S(2)}) collective-permute-start(bf16[48,384]{1,0:T(8,128)(2,1)S(1)} %collective-permute-done.3), channel_id=1, source_target_pairs={{0,120},{8,0},{16,8},{24,16},{32,24},{40,32},{48,40},{56,48},{64,5... | collective-permute-start | bytes 110600 | tf_op jit(solution)/shard_map/ppermute | solution.py:21
  107.3 7.3 %collective-permute-start.4 = (bf16[48,384]{1,0:T(8,128)(2,1)S(1)}, bf16[48,384]{1,0:T(8,128)(2,1)S(1)}, u32[]{:S(2)}, u32[]{:S(2)}) collective-permute-start(bf16[48,384]{1,0:T(8,128)(2,1)S(1)} %collective-permute-done.2), channel_id=1, source_target_pairs={{0,8},{8,16},{16,24},{24,32},{32,40},{40,48},{48,56},{56,64},{64,7... | collective-permute-start | bytes 110600 | tf_op jit(solution)/shard_map/ppermute | solution.py:18
  108.9 7.3 %collective-permute-start.7 = (bf16[48,384]{1,0:T(8,128)(2,1)S(1)}, bf16[48,384]{1,0:T(8,128)(2,1)S(1)}, u32[]{:S(2)}, u32[]{:S(2)}) collective-permute-start(bf16[48,384]{1,0:T(8,128)(2,1)S(1)} %collective-permute-done.5), channel_id=1, source_target_pairs={{0,120},{8,0},{16,8},{24,16},{32,24},{40,32},{48,40},{56,48},{64,5... | collective-permute-start | bytes 110600 | tf_op jit(solution)/shard_map/ppermute | solution.py:21
  114.6 7.3 %collective-permute-start.6 = (bf16[48,384]{1,0:T(8,128)(2,1)S(1)}, bf16[48,384]{1,0:T(8,128)(2,1)S(1)}, u32[]{:S(2)}, u32[]{:S(2)}) collective-permute-start(bf16[48,384]{1,0:T(8,128)(2,1)S(1)} %collective-permute-done.4), channel_id=1, source_target_pairs={{0,8},{8,16},{16,24},{24,32},{32,40},{40,48},{48,56},{56,64},{64,7... | collective-permute-start | bytes 110600 | tf_op jit(solution)/shard_map/ppermute | solution.py:18
  116.2 7.3 %collective-permute-start.9 = (bf16[48,384]{1,0:T(8,128)(2,1)S(1)}, bf16[48,384]{1,0:T(8,128)(2,1)S(1)}, u32[]{:S(2)}, u32[]{:S(2)}) collective-permute-start(bf16[48,384]{1,0:T(8,128)(2,1)S(1)} %collective-permute-done.7), channel_id=1, source_target_pairs={{0,120},{8,0},{16,8},{24,16},{32,24},{40,32},{48,40},{56,48},{64,5... | collective-permute-start | bytes 110600 | tf_op jit(solution)/shard_map/ppermute | solution.py:21
  121.9 7.3 %collective-permute-start.8 = (bf16[48,384]{1,0:T(8,128)(2,1)S(1)}, bf16[48,384]{1,0:T(8,128)(2,1)S(1)}, u32[]{:S(2)}, u32[]{:S(2)}) collective-permute-start(bf16[48,384]{1,0:T(8,128)(2,1)S(1)} %collective-permute-done.6), channel_id=1, source_target_pairs={{0,8},{8,16},{16,24},{24,32},{32,40},{40,48},{48,56},{56,64},{64,7... | collective-permute-start | bytes 110600 | tf_op jit(solution)/shard_map/ppermute | solution.py:18
  123.5 7.3 %collective-permute-start.11 = (bf16[48,384]{1,0:T(8,128)(2,1)S(1)}, bf16[48,384]{1,0:T(8,128)(2,1)S(1)}, u32[]{:S(2)}, u32[]{:S(2)}) collective-permute-start(bf16[48,384]{1,0:T(8,128)(2,1)S(1)} %collective-permute-done.9), channel_id=1, source_target_pairs={{0,120},{8,0},{16,8},{24,16},{32,24},{40,32},{48,40},{56,48},{64,5... | collective-permute-start | bytes 110600 | tf_op jit(solution)/shard_map/ppermute | solution.py:21
  129.2 7.3 %collective-permute-start.10 = (bf16[48,384]{1,0:T(8,128)(2,1)S(1)}, bf16[48,384]{1,0:T(8,128)(2,1)S(1)}, u32[]{:S(2)}, u32[]{:S(2)}) collective-permute-start(bf16[48,384]{1,0:T(8,128)(2,1)S(1)} %collective-permute-done.8), channel_id=1, source_target_pairs={{0,8},{8,16},{16,24},{24,32},{32,40},{40,48},{48,56},{56,64},{64,7... | collective-permute-start | bytes 110600 | tf_op jit(solution)/shard_map/ppermute | solution.py:18
  130.8 13.5 %collective-permute-start.13 = (bf16[48,384]{1,0:T(8,128)(2,1)S(1)}, bf16[48,384]{1,0:T(8,128)(2,1)S(1)}, u32[]{:S(2)}, u32[]{:S(2)}) collective-permute-start(bf16[48,384]{1,0:T(8,128)(2,1)S(1)} %collective-permute-done.11), channel_id=1, source_target_pairs={{0,120},{8,0},{16,8},{24,16},{32,24},{40,32},{48,40},{56,48},{64,5... | collective-permute-start | bytes 110600 | tf_op jit(solution)/shard_map/ppermute | solution.py:21
  136.4 7.3 %collective-permute-start.12 = (bf16[48,384]{1,0:T(8,128)(2,1)S(1)}, bf16[48,384]{1,0:T(8,128)(2,1)S(1)}, u32[]{:S(2)}, u32[]{:S(2)}) collective-permute-start(bf16[48,384]{1,0:T(8,128)(2,1)S(1)} %collective-permute-done.10), channel_id=1, source_target_pairs={{0,8},{8,16},{16,24},{24,32},{32,40},{40,48},{48,56},{56,64},{64,7... | collective-permute-start | bytes 110600 | tf_op jit(solution)/shard_map/ppermute | solution.py:18
  143.7 7.3 %collective-permute-start.14 = (bf16[48,384]{1,0:T(8,128)(2,1)S(1)}, bf16[48,384]{1,0:T(8,128)(2,1)S(1)}, u32[]{:S(2)}, u32[]{:S(2)}) collective-permute-start(bf16[48,384]{1,0:T(8,128)(2,1)S(1)} %collective-permute-done.12), channel_id=1, source_target_pairs={{0,8},{8,16},{16,24},{24,32},{32,40},{40,48},{48,56},{56,64},{64,7... | collective-permute-start | bytes 110600 | tf_op jit(solution)/shard_map/ppermute | solution.py:18
  171.6 140.8 %all-reduce.4.cloned.1.call-start = ((), (), s32[]{:S(2)}) async-start(), calls=%async_computation.3 | async-start | bytes 3735552 | tf_op jit(solution)/shard_map/psum | solution.py:162
  174.4 5.1 %copy-start.13 = (bf16[256,384]{0,1:T(8,128)(2,1)S(1)}, bf16[256,384]{0,1:T(8,128)(2,1)}, u32[]{:S(2)}) copy-start(bf16[256,384]{0,1:T(8,128)(2,1)} %copy.85) | copy-start | bytes 589828
  247.5 182.9 %reduce-scatter.5.cloned.1.call-start = ((), (), s32[]{:S(2)}) async-start(), calls=%async_computation.4 | async-start | bytes 4423680 | tf_op jit(solution)/shard_map/reduce_scatter | solution.py:172
  371.0 8.9 %copy-start.23 = (bf16[3072,512]{1,0:T(8,128)(2,1)S(1)}, bf16[3072,512]{1,0:T(8,128)(2,1)}, u32[]{:S(2)}) copy-start(bf16[3072,512]{1,0:T(8,128)(2,1)} %param.33) | copy-start | bytes 9437188
  (18 other events, 51.0 us)
Sparse Core Ops, SparseCore 0:
  171.7 70.1 reduce-scatter.6
  247.7 64.6 all-reduce.3
  393.0 37.3 reduce-scatter.4
